TPU v7x, 32 devices: a whole 2x2x4 slice. The times are simulated.
32 devices in a mesh: dp: 8 (over z, y), tensor: 4 (over x, core).
Axes of the slice: x: 2, y: 2, z: 4, core: 2. Of those that a mesh axis runs over, the one named last changes fastest.
Arguments:
- hidden_in: bfloat16 [32768, 768], P(('dp', 'tensor')), may hold values from -6 to 6
- qkv_weight: bfloat16 [3, 768, 768], P(None, 'tensor'), may hold values from -0.21875 to 0.21875
- qv_bias: bfloat16 [2, 768], P(None, 'tensor'), may hold values from -3 to 3
- out_weight: bfloat16 [768, 768], P('tensor'), may hold values from -1.25 to 1.25
- out_bias: bfloat16 [768], replicated, may hold values from -3 to 3
- norm1_gain: bfloat16 [768], replicated, may hold values from 0.25 to 1.75
- norm1_shift: bfloat16 [768], replicated, may hold values from -3 to 3
- up_weight: bfloat16 [3072, 768], P('tensor'), may hold values from -0.21875 to 0.21875
- up_bias: bfloat16 [3072], P('tensor'), may hold values from -3 to 3
- down_weight: bfloat16 [3072, 768], P('tensor'), may hold values from -0.109375 to 0.109375
- down_bias: bfloat16 [768], replicated, may hold values from -3 to 3
- norm2_gain: bfloat16 [768], replicated, may hold values from 0.25 to 1.75
- norm2_shift: bfloat16 [768], replicated, may hold values from -3 to 3
- out_grad: bfloat16 [32768, 768], P(('dp', 'tensor')), may hold values from -12 to 12
- seq_lengths: int32 [256], P('dp'), may hold values from 32 to 128, as said below
- key_mask: int32 [32768], P('dp'), may hold values 0 or 1
- split_pos: int32 [256], P('dp'), may hold values from 8 to 95, as said below
Outputs:
- layer_out: bfloat16 [32768, 768], P(('dp', 'tensor'))
- input_grad: bfloat16 [32768, 768], P(('dp', 'tensor'))
- grad_qkv_weight: float32 [3, 768, 768], P(None, 'tensor')
- grad_qv_bias: float32 [2, 768], P(None, 'tensor')
- grad_out_weight: float32 [768, 768], P('tensor')
- grad_out_bias: float32 [768], replicated
- grad_norm1_gain: float32 [768], replicated
- grad_norm1_shift: float32 [768], replicated
- grad_up_weight: float32 [3072, 768], P('tensor')
- grad_up_bias: float32 [3072], P('tensor')
- grad_down_weight: float32 [3072, 768], P('tensor')
- grad_down_bias: float32 [768], replicated
- grad_norm2_gain: float32 [768], replicated
- grad_norm2_shift: float32 [768], replicated
Inputs may be any that keep to these rules, and one draw needn't show every extreme that they name: `seq_lengths`: every slot's length is at least a quarter of 128; the first slot of each index of dp is full. `split_pos`: a slot's split position is at least its length // 4 (a quarter, rounded down) and below three quarters of it.
All inputs are finite; a program needn't handle non-finite values. No bound on the sum of `key_mask` on one device may be relied on, other than what follows from the above.
Results may differ from a plain program's by a relative error of at most 0.019.
Values may be sent and summed in bfloat16 or wider, within the bound.
No kernel may reach another device: no remote copies, remote signals or barrier semaphores. Data moves between devices by JAX's collectives and lax.ppermute only.
A program may use at most 192 MiB of HBM per device.

v0:
```python
import jax
import jax.numpy as jnp
from jax import lax
from jax.sharding import PartitionSpec as P

HD = 64


EPSILON = 1e-05
ROOT_HALF = 0.7071067811865476
DENSITY = 0.3989422804014327


def norm_forward(hidden, norm_gain, norm_offset):
    average = jnp.mean(hidden, axis=1, keepdims=True)
    centred = hidden - average
    spread = jnp.mean(centred * centred, axis=1, keepdims=True)
    inverse = lax.rsqrt(spread + EPSILON)
    normal = centred * inverse
    return (normal * norm_gain + norm_offset, normal, inverse)


def norm_backward(upstream, normal, inverse, norm_gain):
    scaled = upstream * norm_gain
    first_mean = jnp.mean(scaled, axis=1, keepdims=True)
    second_mean = jnp.mean(scaled * normal, axis=1, keepdims=True)
    return inverse * (scaled - first_mean - normal * second_mean)


def gelu_parts(before):
    cumulative = 0.5 * (1.0 + jax.scipy.special.erf(before * ROOT_HALF))
    density = DENSITY * jnp.exp(-0.5 * before * before)
    return (before * cumulative, cumulative + before * density)


def score_block(queries, key_rows, valid_keys):
    raw_scores = jnp.einsum(
        "bqhe,bkhe->bhqk", queries, key_rows, preferred_element_type=jnp.float32
    ) * HD ** (-0.5)
    return jnp.where(valid_keys[:, None, None, :], raw_scores, -1e30)


def attend_forward(operands):
    queries, key_rows, value_rows, valid_keys = operands
    masked = score_block(queries, key_rows, valid_keys)
    largest = jnp.max(masked, axis=-1, keepdims=True)
    weights_raw = jnp.exp(masked - largest)
    totals = jnp.sum(weights_raw, axis=-1, keepdims=True)
    probability = weights_raw / totals
    log_total = largest + jnp.log(totals)
    context = jnp.einsum(
        "bhqk,bkhe->bqhe",
        probability.astype(jnp.bfloat16),
        value_rows,
        preferred_element_type=jnp.float32,
    )
    return (context.astype(jnp.bfloat16), log_total)


def attend_backward(operands):
    queries, key_rows, value_rows, valid_keys, log_total, context_grad = operands
    masked = score_block(queries, key_rows, valid_keys)
    probability = jnp.exp(masked - log_total)
    value_grad = jnp.einsum(
        "bhqk,bqhe->bkhe",
        probability.astype(jnp.bfloat16),
        context_grad,
        preferred_element_type=jnp.float32,
    )
    prob_grad = jnp.einsum(
        "bqhe,bkhe->bhqk", context_grad, value_rows, preferred_element_type=jnp.float32
    )
    inner_sum = jnp.sum(probability * prob_grad, axis=-1, keepdims=True)
    score_grad = (probability * (prob_grad - inner_sum)).astype(jnp.bfloat16)
    query_grad = jnp.einsum(
        "bhqk,bkhe->bqhe", score_grad, key_rows, preferred_element_type=jnp.float32
    ) * HD ** (-0.5)
    key_grad = jnp.einsum(
        "bhqk,bqhe->bkhe", score_grad, queries, preferred_element_type=jnp.float32
    ) * HD ** (-0.5)
    return (query_grad, key_grad, value_grad)


def body(
    hidden_in,
    qkv_weight,
    qv_bias,
    out_weight,
    out_bias,
    norm1_gain,
    norm1_shift,
    up_weight,
    up_bias,
    down_weight,
    down_bias,
    norm2_gain,
    norm2_shift,
    out_grad,
    seq_lengths,
    key_mask,
    split_pos,
):
    shard_rows = hidden_in.shape[0]
    part_count = lax.axis_size("tensor")
    part_index = lax.axis_index("tensor")
    group_rows = shard_rows * part_count
    slot_count = seq_lengths.shape[0]
    slot_len = group_rows // slot_count
    local_width = qkv_weight.shape[1]
    local_heads = local_width // HD
    per_block = max(1, min(slot_count, 512 // slot_len))
    block_count = slot_count // per_block
    shard_slots = slot_count // part_count
    places = lax.broadcasted_iota(jnp.int32, (slot_count, slot_len), 1)
    valid_keys = (places < seq_lengths[:, None]) & (
        (key_mask.reshape(slot_count, slot_len) == 1) | (places == 0)
    )
    valid_blocks = valid_keys.reshape(block_count, per_block, slot_len)
    own_lengths = lax.dynamic_slice_in_dim(seq_lengths, part_index * shard_slots, shard_slots)
    own_splits = lax.dynamic_slice_in_dim(split_pos, part_index * shard_slots, shard_slots)
    own_places = places[:shard_slots]
    target = (
        ((own_places >= own_splits[:, None]) & (own_places < own_lengths[:, None]))
        .astype(jnp.float32)
        .reshape(shard_rows, 1)
    )
    gain_mid = norm1_gain.astype(jnp.float32)
    shift_mid = norm1_shift.astype(jnp.float32)
    gain_out = norm2_gain.astype(jnp.float32)
    shift_out = norm2_shift.astype(jnp.float32)
    gathered = lax.all_gather(hidden_in, "tensor", axis=0, tiled=True)
    projected = jnp.einsum("rd,cld->crl", gathered, qkv_weight, preferred_element_type=jnp.float32)
    zero_bias = jnp.zeros_like(qv_bias[0])
    projected = (
        projected + jnp.stack([qv_bias[0], zero_bias, qv_bias[1]]).astype(jnp.float32)[:, None, :]
    )
    projected = projected.astype(jnp.bfloat16)
    head_shape = (block_count, per_block, slot_len, local_heads, HD)
    queries = projected[0].reshape(head_shape)
    key_rows = projected[1].reshape(head_shape)
    value_rows = projected[2].reshape(head_shape)
    context, log_total = lax.map(attend_forward, (queries, key_rows, value_rows, valid_blocks))
    context_rows = context.reshape(group_rows, local_width)
    attn_out = lax.psum_scatter(
        jnp.dot(context_rows, out_weight, preferred_element_type=jnp.float32).astype(jnp.bfloat16),
        "tensor",
        scatter_dimension=0,
        tiled=True,
    ).astype(jnp.float32)
    first_sum = hidden_in.astype(jnp.float32) + attn_out + out_bias.astype(jnp.float32)
    mid_rows, mid_normal, mid_inverse = norm_forward(first_sum, gain_mid, shift_mid)
    mid_low = mid_rows.astype(jnp.bfloat16)
    mid_all = lax.all_gather(mid_low, "tensor", axis=0, tiled=True)
    before = jnp.einsum(
        "rd,fd->rf", mid_all, up_weight, preferred_element_type=jnp.float32
    ) + up_bias.astype(jnp.float32)
    activated, gelu_slope = gelu_parts(before)
    activated_low = activated.astype(jnp.bfloat16)
    ffn_out = lax.psum_scatter(
        jnp.dot(activated_low, down_weight, preferred_element_type=jnp.float32).astype(
            jnp.bfloat16
        ),
        "tensor",
        scatter_dimension=0,
        tiled=True,
    ).astype(jnp.float32)
    second_sum = mid_rows + ffn_out + down_bias.astype(jnp.float32)
    out_rows, out_normal, out_inverse = norm_forward(second_sum, gain_out, shift_out)
    layer_out = out_rows.astype(jnp.bfloat16)
    upstream = out_grad.astype(jnp.float32) * target
    grad_gain_out = jnp.sum(upstream * out_normal, axis=0)
    grad_shift_out = jnp.sum(upstream, axis=0)
    second_grad = norm_backward(upstream, out_normal, out_inverse, gain_out)
    grad_down_bias = jnp.sum(second_grad, axis=0)
    second_low = second_grad.astype(jnp.bfloat16)
    second_all = lax.all_gather(second_low, "tensor", axis=0, tiled=True)
    grad_down = jnp.einsum(
        "rf,rd->fd", activated_low, second_all, preferred_element_type=jnp.float32
    )
    activated_grad = jnp.einsum(
        "rd,fd->rf", second_all, down_weight, preferred_element_type=jnp.float32
    )
    before_low = (activated_grad * gelu_slope).astype(jnp.bfloat16)
    grad_up = jnp.einsum("rf,rd->fd", before_low, mid_all, preferred_element_type=jnp.float32)
    grad_up_bias = jnp.sum(before_low, axis=0, dtype=jnp.float32)
    mid_grad_part = lax.psum_scatter(
        jnp.dot(before_low, up_weight, preferred_element_type=jnp.float32).astype(jnp.bfloat16),
        "tensor",
        scatter_dimension=0,
        tiled=True,
    ).astype(jnp.float32)
    mid_grad = second_grad + mid_grad_part
    grad_gain_mid = jnp.sum(mid_grad * mid_normal, axis=0)
    grad_shift_mid = jnp.sum(mid_grad, axis=0)
    first_grad = norm_backward(mid_grad, mid_normal, mid_inverse, gain_mid)
    grad_out_bias = jnp.sum(first_grad, axis=0)
    first_low = first_grad.astype(jnp.bfloat16)
    first_all = lax.all_gather(first_low, "tensor", axis=0, tiled=True)
    grad_out_weight = jnp.einsum(
        "rl,rd->ld", context_rows, first_all, preferred_element_type=jnp.float32
    )
    context_grad = (
        jnp.einsum("rd,ld->rl", first_all, out_weight, preferred_element_type=jnp.float32)
        .astype(jnp.bfloat16)
        .reshape(head_shape)
    )
    query_grad, key_grad, value_grad = lax.map(
        attend_backward, (queries, key_rows, value_rows, valid_blocks, log_total, context_grad)
    )
    projected_grad = jnp.stack(
        [
            query_grad.reshape(group_rows, local_width),
            key_grad.reshape(group_rows, local_width),
            value_grad.reshape(group_rows, local_width),
        ]
    ).astype(jnp.bfloat16)
    grad_qkv = jnp.einsum(
        "crl,rd->cld", projected_grad, gathered, preferred_element_type=jnp.float32
    )
    bias_sums = jnp.sum(projected_grad, axis=1, dtype=jnp.float32)
    grad_qv_bias = jnp.stack([bias_sums[0], bias_sums[2]])
    input_part = lax.psum_scatter(
        jnp.einsum(
            "crl,cld->rd", projected_grad, qkv_weight, preferred_element_type=jnp.float32
        ).astype(jnp.bfloat16),
        "tensor",
        scatter_dimension=0,
        tiled=True,
    ).astype(jnp.float32)
    input_grad = (first_grad + input_part).astype(jnp.bfloat16)
    grad_qkv, grad_qv_bias, grad_out_weight, grad_up, grad_up_bias, grad_down = lax.psum(
        (grad_qkv, grad_qv_bias, grad_out_weight, grad_up, grad_up_bias, grad_down), "dp"
    )
    grad_out_bias, grad_gain_mid, grad_shift_mid, grad_down_bias, grad_gain_out, grad_shift_out = (
        lax.psum(
            (
                grad_out_bias,
                grad_gain_mid,
                grad_shift_mid,
                grad_down_bias,
                grad_gain_out,
                grad_shift_out,
            ),
            ("dp", "tensor"),
        )
    )
    return (
        layer_out,
        input_grad,
        grad_qkv,
        grad_qv_bias,
        grad_out_weight,
        grad_out_bias,
        grad_gain_mid,
        grad_shift_mid,
        grad_up,
        grad_up_bias,
        grad_down,
        grad_down_bias,
        grad_gain_out,
        grad_shift_out,
    )


def solution(mesh):
    in_specs = (
        P(("dp", "tensor"), None),
        P(None, "tensor", None),
        P(None, "tensor"),
        P("tensor", None),
        P(),
        P(),
        P(),
        P("tensor", None),
        P("tensor"),
        P("tensor", None),
        P(),
        P(),
        P(),
        P(("dp", "tensor"), None),
        P("dp"),
        P("dp"),
        P("dp"),
    )
    out_specs = (
        P(("dp", "tensor"), None),
        P(("dp", "tensor"), None),
        P(None, "tensor", None),
        P(None, "tensor"),
        P("tensor", None),
        P(),
        P(),
        P(),
        P("tensor", None),
        P("tensor"),
        P("tensor", None),
        P(),
        P(),
        P(),
    )
    return jax.shard_map(body, mesh=mesh, in_specs=in_specs, out_specs=out_specs, check_vma=False)
```

profile of v0, /device:TPU:0, one launch (start us, length us, event | category | flops | bytes accessed | tf_op | source)
XLA Modules:
  0.0 924.1 jit_solution(13614547716441591515)
XLA Ops:
  10.5 48.2 %all-gather.5.cloned.1.call-done = bf16[4096,768]{1,0:T(8,128)(2,1)} async-done(((bf16[1024,768]{1,0:T(8,128)(2,1)}), bf16[4096,768]{1,0:T(8,128)(2,1)}) %all-gather.5.cloned.1.call-update) | async-done | bytes 6291472 | tf_op jit(solution)/shard_map/all_gather | solution.py:131
  58.7 6.9 fusion.48
  85.9 27.9 %while.26 = (s32[]{:T(128)}, bf16[8,4,128,3,64]{2,1,0,4,3:T(4,128)(2,1)}, f32[8,4,3,128,1]{3,2,1,4,0:T(4,128)S(1)}, bf16[8,4,128,3,64]{2,4,3,1,0:T(8,128)(2,1)},...) while((s32[]{:T(128)}, ...), condition=%wide.region_3.4_spmd, body=%wide.region_0.3_spmd.sunk | while | flops 52001280 | bytes 3597917 | solution.py:142
  118.2 5.9 convolution_convert_fusion.1
  124.8 58.3 %reduce-scatter.5.cloned.1.call-done = bf16[1024,768]{1,0:T(8,128)(2,1)} async-done(((bf16[4096,768]{1,0:T(8,128)(2,1)}), bf16[1024,768]{1,0:T(8,128)(2,1)}) %reduce-scatter.5.cloned.1.call-update) | async-done | bytes 1572880 | tf_op jit(solution)/shard_map/reduce_scatter | solution.py:144
  188.3 46.4 %all-gather.7.cloned.1.call-done = bf16[4096,768]{1,0:T(8,128)(2,1)} async-done(((bf16[1024,768]{1,0:T(8,128)(2,1)}), bf16[4096,768]{1,0:T(8,128)(2,1)}) %all-gather.7.cloned.1.call-update) | async-done | bytes 6291472 | tf_op jit(solution)/shard_map/all_gather | solution.py:153
  234.8 11.1 %multiply_convert_fusion.1 = (bf16[4096,768]{1,0:T(8,128)(2,1)S(1)}, f32[4096,768]{1,0:T(8,128)}) fusion(f32[768]{0:T(1024)S(1)} %convert_element_type.130, bf16[4096,768]{1,0:T(8,128)(2,1)} %all-gather.7.cloned.1.call-done, bf16[768,768]{1,0:T(8,128)(2,1)S(1)} %copy-done), kind=kOutput, calls=%fused_computation.62 | convolution fusion | flops 4850712576 | bytes 26348544 | tf_op jit(solution)/shard_map/rd,fd->rf/dot_general | solution.py:154
  248.6 7.1 convolution_convert_fusion.3
  256.6 58.1 %reduce-scatter.7.cloned.1.call-done = bf16[1024,768]{1,0:T(8,128)(2,1)} async-done(((bf16[4096,768]{1,0:T(8,128)(2,1)}), bf16[1024,768]{1,0:T(8,128)(2,1)}) %reduce-scatter.7.cloned.1.call-update) | async-done | bytes 1572880 | tf_op jit(solution)/shard_map/reduce_scatter | solution.py:159
  324.8 46.3 %all-gather.9.cloned.1.call-done = bf16[4096,768]{1,0:T(8,128)(2,1)} async-done(((bf16[1024,768]{1,0:T(8,128)(2,1)}), bf16[4096,768]{1,0:T(8,128)(2,1)}) %all-gather.9.cloned.1.call-update) | async-done | bytes 6291472 | tf_op jit(solution)/shard_map/all_gather | solution.py:176
  371.1 12.2 %convert_reduce_fusion = (f32[768]{0:T(1024)S(1)}, bf16[4096,768]{1,0:T(8,128)(2,1)S(1)}) fusion(f32[4096,768]{1,0:T(8,128)} %get-tuple-element.219, f32[768]{0:T(1024)S(1)} %convert_element_type.130, bf16[4096,768]{1,0:T(8,128)(2,1)} %all-gather.9.cloned.1.call-done, bf16[768,768]{1,0:T(8,128)(2,1)} %param.30), kind=kOutput, calls=%fused_computation.61 | convolution fusion | flops 4872731648 | bytes 26351616 | tf_op jit(solution)/shard_map/rd,fd->rf/dot_general | solution.py:180
  385.9 7.0 convolution_convert_fusion.2
  393.0 58.9 %reduce-scatter.9.cloned.1.call-done = bf16[1024,768]{1,0:T(8,128)(2,1)} async-done(((bf16[4096,768]{1,0:T(8,128)(2,1)}), bf16[1024,768]{1,0:T(8,128)(2,1)}) %reduce-scatter.9.cloned.1.call-update) | async-done | bytes 1572880 | tf_op jit(solution)/shard_map/reduce_scatter | solution.py:186
  452.0 4.8 multiply_reduce_fusion.2
  461.8 46.2 %all-gather.11.cloned.1.call-done = bf16[4096,768]{1,0:T(8,128)(2,1)} async-done(((bf16[1024,768]{1,0:T(8,128)(2,1)}), bf16[4096,768]{1,0:T(8,128)(2,1)}) %all-gather.11.cloned.1.call-update) | async-done | bytes 6291472 | tf_op jit(solution)/shard_map/all_gather | solution.py:198
  508.0 6.1 convolution_convert_fusion.4
  517.0 62.5 %while.27 = (s32[]{:T(128)}, bf16[8,4,128,3,64]{2,4,3,1,0:T(8,128)(2,1)}, bf16[8,4,128,3,64]{2,4,3,1,0:T(8,128)(2,1)}, bf16[8,4,128,3,64]{2,4,3,1,0:T(8,128)(2,1...) while((s32[]{:T(128)}, ...), condition=%wide.region_17.18_spmd, body=%wide.region_15.17_spmd.sunk | while | flops 127793664 | bytes 8883833 | solution.py:207
  603.4 9.5 %bitcast_convert_fusion = bf16[4096,768]{1,0:T(8,128)(2,1)} fusion(bf16[3,4096,192]{1,2,0:T(8,128)(2,1)} %constant_dynamic-update-slice_fusion, bf16[3,192,768]{2,1,0:T(8,128)(2,1)S(1)} %copy-done.26), kind=kOutput, calls=%fused_computation.60 | convolution fusion | flops 3627024384 | bytes 11894784 | tf_op jit(solution)/shard_map/crl,cld->rd/dot_general | solution.py:223
  613.2 10.2 %fusion.68 = f32[768,768]{1,0:T(8,128)} fusion(bf16[4096,768]{1,0:T(8,128)(2,1)} %copy-done.28, bf16[4096,768]{1,0:T(8,128)(2,1)} %all-gather.9.cloned.1.call-done), kind=kOutput, calls=%fused_computation.129 | convolution fusion | flops 4831838208 | bytes 14942208 | tf_op jit(solution)/shard_map/rf,rd->fd/dot_general | solution.py:177
  623.4 10.8 %fusion.67 = f32[768,768]{1,0:T(8,128)} fusion(bf16[4096,768]{1,0:T(8,128)(2,1)} %copy-done.29, bf16[4096,768]{1,0:T(8,128)(2,1)} %all-gather.7.cloned.1.call-done), kind=kOutput, calls=%fused_computation.128 | convolution fusion | flops 4831838208 | bytes 14942208 | tf_op jit(solution)/shard_map/rf,rd->fd/dot_general | solution.py:184
  636.5 5.0 fusion.42
  641.5 41.1 %all-reduce = (f32[768]{0:T(1024)}, f32[768]{0:T(1024)}, f32[768]{0:T(1024)}, f32[768]{0:T(1024)}, f32[768]{0:T(1024)}, /*index=5*/f32[768]{0:T(1024)}) all-reduce(f32[768]{0:T(1024)S(1)} %get-tuple-element.200, f32[768]{0:T(1024)S(1)} %get-tuple-element.145, ...), channel_id=1, replica_groups=mesh['dp'=8,'tensor'=4] {'dp','tensor'}, use_global_device_ids=true, to_apply=%region_24.25 | all-reduce | flops 4608 | bytes 36864 | tf_op jit(solution)/shard_map/psum | solution.py:235
  686.5 23.8 %all-reduce.1 = (f32[2,192]{1,0:T(2,128)}, f32[768]{0:T(1024)}) all-reduce(f32[2,192]{1,0:T(2,128)S(1)} %pad_maximum_fusion, f32[768]{0:T(1024)S(1)} %get-tuple-element.220), channel_id=1, replica_groups=mesh['dp'=8,'tensor'=4] {'dp'}, use_global_device_ids=true, to_apply=%region_21.22 | all-reduce | flops 1152 | bytes 9216 | tf_op jit(solution)/shard_map/psum | solution.py:231
  714.2 196.4 %all-reduce.5.cloned.1.call-done = (f32[3,192,768]{2,1,0:T(8,128)}, f32[192,768]{1,0:T(8,128)}, f32[768,768]{1,0:T(8,128)}, f32[768,768]{1,0:T(8,128)}) async-done(((f32[3,192,768]{2,1,0:T(8,128)}, f32[192,768]{1,0:T(8,128)}, f32[768,768]{1,0:T(8,128)}, f32[768,768]{1,0:T(8,128)}), (f32[3,192,768]{2,1,0:T(8,128)}, f32[192,768]{1,0:T(8,128)}, f32[768,768]{1,0:T(8,128)}, ...) | async-done | bytes 7077904 | tf_op jit(solution)/shard_map/psum | solution.py:231
  (279 shorter events, 188.3 us)
Async XLA Ops:
  7.2 227.6 %copy-start = (bf16[768,768]{1,0:T(8,128)(2,1)S(1)}, bf16[768,768]{1,0:T(8,128)(2,1)}, u32[]{:S(2)}) copy-start(bf16[768,768]{1,0:T(8,128)(2,1)} %param.28) | copy-start | bytes 3538948
  7.2 51.5 %all-gather.5.cloned.1.call-start = ((), (), s32[]{:S(2)}) async-start(), calls=%async_computation.4 | async-start | bytes 7864320 | tf_op jit(solution)/shard_map/all_gather | solution.py:131
  7.9 175.2 %reduce-scatter.5.cloned.1.call-start = ((), (), s32[]{:S(2)}) async-start(), calls=%async_computation.5 | async-start | bytes 7864320 | tf_op jit(solution)/shard_map/reduce_scatter | solution.py:144
  113.9 10.2 %copy-start.7 = (bf16[8,4,128,3,64]{2,4,3,1,0:T(8,128)(2,1)}, bf16[8,4,128,3,64]{2,4,3,1,0:T(8,128)(2,1)S(1)}, u32[]{:S(2)}) copy-start(bf16[8,4,128,3,64]{2,4,3,1,0:T(8,128)(2,1)S(1)} %get-tuple-element.428) | copy-start | bytes 4718596
  113.9 4.3 copy-start.16
  124.1 59.0 %copy-start.2 = (bf16[1024,768]{1,0:T(8,128)(2,1)S(1)}, bf16[1024,768]{1,0:T(8,128)(2,1)}, u32[]{:S(2)}) copy-start(bf16[1024,768]{1,0:T(8,128)(2,1)} %param.21) | copy-start | bytes 4718596
  124.2 110.6 %all-gather.7.cloned.1.call-start = ((), (), s32[]{:S(2)}) async-start(), calls=%async_computation.6 | async-start | bytes 7864320 | tf_op jit(solution)/shard_map/all_gather | solution.py:153
  188.3 126.4 %reduce-scatter.7.cloned.1.call-start = ((), (), s32[]{:S(2)}) async-start(), calls=%async_computation.7 | async-start | bytes 7864320 | tf_op jit(solution)/shard_map/reduce_scatter | solution.py:159
  234.8 13.8 %copy-start.25 = (bf16[768,768]{1,0:T(8,128)(2,1)S(1)}, bf16[768,768]{1,0:T(8,128)(2,1)}, u32[]{:S(2)}) copy-start(bf16[768,768]{1,0:T(8,128)(2,1)} %param.30) | copy-start | bytes 3538948
  255.7 115.4 %all-gather.9.cloned.1.call-start = ((), (), s32[]{:S(2)}) async-start(), calls=%async_computation.8 | async-start | bytes 7864320 | tf_op jit(solution)/shard_map/all_gather | solution.py:176
  324.6 127.4 %reduce-scatter.9.cloned.1.call-start = ((), (), s32[]{:S(2)}) async-start(), calls=%async_computation.9 | async-start | bytes 7864320 | tf_op jit(solution)/shard_map/reduce_scatter | solution.py:186
  393.0 115.1 %all-gather.11.cloned.1.call-start = ((), (), s32[]{:S(2)}) async-start(), calls=%async_computation.10 | async-start | bytes 7864320 | tf_op jit(solution)/shard_map/all_gather | solution.py:198
  452.0 4.9 copy-start.4
  452.0 4.9 copy-start.6
  452.0 4.9 copy-start.10
  461.5 248.8 %reduce-scatter.11.cloned.1.call-start = ((), (), s32[]{:S(2)}) async-start(), calls=%async_computation.11 | async-start | bytes 7864320 | tf_op jit(solution)/shard_map/reduce_scatter | solution.py:222
  612.8 297.7 %all-reduce.5.cloned.1.call-start = ((), (), s32[]{:S(2)}) async-start(), calls=%async_computation.12 | async-start | bytes 14155776 | tf_op jit(solution)/shard_map/psum | solution.py:231
  613.2 21.1 %slice-start.4 = ((s8[6291456]{0:T(1024)(128)(4,1)}), s8[4194304]{0:T(1024)(128)(4,1)S(1)}, s32[]{:S(2)}) async-start(s8[6291456]{0:T(1024)(128)(4,1)} %bitcast.166), calls=%async_computation.17 | async-start | bytes 8388608
  613.2 23.3 %slice-start = ((s8[4718592]{0:T(1024)(128)(4,1)}), s8[4194304]{0:T(1024)(128)(4,1)S(1)}, s32[]{:S(2)}) async-start(s8[4718592]{0:T(1024)(128)(4,1)} %bitcast.161), calls=%async_computation.13 | async-start | bytes 8388608
  613.2 23.3 %slice-start.2 = ((s8[6291456]{0:T(1024)(128)(4,1)}), s8[4194304]{0:T(1024)(128)(4,1)S(1)}, s32[]{:S(2)}) async-start(s8[6291456]{0:T(1024)(128)(4,1)} %bitcast.164), calls=%async_computation.15 | async-start | bytes 8388608
  623.4 10.9 %copy-start.8 = (bf16[4096,192]{0,1:T(8,128)(2,1)S(1)}, bf16[4096,192]{0,1:T(8,128)(2,1)}, u32[]{:S(2)}) copy-start(bf16[4096,192]{0,1:T(8,128)(2,1)} %reshape.182) | copy-start | bytes 4718596
  623.4 10.9 %slice-start.5 = ((s8[6291456]{0:T(1024)(128)(4,1)}), s8[2097152]{0:T(1024)(128)(4,1)S(1)}, s32[]{:S(2)}) async-start(s8[6291456]{0:T(1024)(128)(4,1)} %bitcast.166), calls=%async_computation.18 | async-start | bytes 4194304
  623.4 13.1 %slice-start.1 = ((s8[4718592]{0:T(1024)(128)(4,1)}), s8[524288]{0:T(1024)(128)(4,1)S(1)}, s32[]{:S(2)}) async-start(s8[4718592]{0:T(1024)(128)(4,1)} %bitcast.161), calls=%async_computation.14 | async-start | bytes 1048576
  623.4 13.1 %slice-start.3 = ((s8[6291456]{0:T(1024)(128)(4,1)}), s8[2097152]{0:T(1024)(128)(4,1)S(1)}, s32[]{:S(2)}) async-start(s8[6291456]{0:T(1024)(128)(4,1)} %bitcast.164), calls=%async_computation.16 | async-start | bytes 4194304
  (21 other events, 38.3 us)
Sparse Core Ops, SparseCore 0:
  9.6 49.0 all-gather.4
  124.3 58.8 reduce-scatter.4
  188.4 46.3 all-gather.6
  255.8 58.8 reduce-scatter.6
  324.7 46.3 all-gather.8
  393.1 58.8 reduce-scatter.8
  461.6 46.3 all-gather.10
  613.0 59.6 reduce-scatter.10
  678.2 232.3 all-reduce.4
where the time goes:
time: 933 us; the launch traced here: 924 us
  waiting for transfers between devices  560 us (60%)
  matrix products  174 us (19%)
  local copies, waits for them, and re-layouts  75.7 us (8%)
  blocking collectives  64.9 us (7%)
  other arithmetic  32.5 us (3%)
  between operations  14.7 us (2%)
    psum x1, waiting for transfers between devices, body(): lax.psum((grad_qkv, grad_qv_bias, grad_out_weight, grad_up, grad_up_bias,...  196 us
    reduce_scatter x1, waiting for transfers between devices, body(): lax.psum_scatter(jnp.dot(before_low, up_weight, preferred_element_type=jn...  58.9 us
    reduce_scatter x1, waiting for transfers between devices, body(): lax.psum_scatter(jnp.dot(context_rows, out_weight, preferred_element_type...  58.3 us
    reduce_scatter x1, waiting for transfers between devices, body(): lax.psum_scatter(jnp.dot(activated_low, down_weight, preferred_element_ty...  58.1 us
    all_gather x1, waiting for transfers between devices, body(): gathered = lax.all_gather(hidden_in, 'tensor', axis=0, tiled=True)  48.2 us
    all_gather x1, waiting for transfers between devices, body(): mid_all = lax.all_gather(mid_low, 'tensor', axis=0, tiled=True)  46.4 us
    all_gather x1, waiting for transfers between devices, body(): second_all = lax.all_gather(second_low, 'tensor', axis=0, tiled=True)  46.3 us
    all_gather x1, waiting for transfers between devices, body(): first_all = lax.all_gather(first_low, 'tensor', axis=0, tiled=True)  46.2 us
  transfers between devices with their start and end apart: 9, of which 8 were waited for; matrix products, arithmetic and copies ran while one was open for 4% of the time, Pallas kernels for 0%

commit v1 on v0

v1 whole, which is shorter than its diff:
```python
import jax
import jax.numpy as jnp
from jax import lax
from jax.sharding import PartitionSpec as P

HD = 64


EPSILON = 1e-05
ROOT_HALF = 0.7071067811865476
DENSITY = 0.3989422804014327
F32 = jnp.float32
BF16 = jnp.bfloat16


def norm_forward(hidden, norm_gain, norm_offset):
    average = jnp.mean(hidden, axis=1, keepdims=True)
    centred = hidden - average
    spread = jnp.mean(centred * centred, axis=1, keepdims=True)
    inverse = lax.rsqrt(spread + EPSILON)
    normal = centred * inverse
    return (normal * norm_gain + norm_offset, normal, inverse)


def norm_backward(upstream, normal, inverse, norm_gain):
    scaled = upstream * norm_gain
    first_mean = jnp.mean(scaled, axis=1, keepdims=True)
    second_mean = jnp.mean(scaled * normal, axis=1, keepdims=True)
    return inverse * (scaled - first_mean - normal * second_mean)


def gelu_parts(before):
    cumulative = 0.5 * (1.0 + jax.scipy.special.erf(before * ROOT_HALF))
    density = DENSITY * jnp.exp(-0.5 * before * before)
    return (before * cumulative, cumulative + before * density)


def body(
    hidden_in,
    qkv_weight,
    qv_bias,
    out_weight,
    out_bias,
    norm1_gain,
    norm1_shift,
    up_weight,
    up_bias,
    down_weight,
    down_bias,
    norm2_gain,
    norm2_shift,
    out_grad,
    seq_lengths,
    key_mask,
    split_pos,
):
    rows = hidden_in.shape[0]
    part_count = lax.axis_size("tensor")
    part_index = lax.axis_index("tensor")
    group_slots = seq_lengths.shape[0]
    slot_len = rows * part_count // group_slots
    slots = rows // slot_len
    width = hidden_in.shape[1]
    heads = width // HD

    w_qkv = lax.all_gather(qkv_weight, "tensor", axis=1, tiled=True)
    b_qv = lax.all_gather(qv_bias, "tensor", axis=1, tiled=True)
    w_out = lax.all_gather(out_weight, "tensor", axis=0, tiled=True)
    w_up = lax.all_gather(up_weight, "tensor", axis=0, tiled=True)
    b_up = lax.all_gather(up_bias, "tensor", axis=0, tiled=True)
    w_down = lax.all_gather(down_weight, "tensor", axis=0, tiled=True)

    lengths = lax.dynamic_slice_in_dim(seq_lengths, part_index * slots, slots)
    splits = lax.dynamic_slice_in_dim(split_pos, part_index * slots, slots)
    mask = lax.dynamic_slice_in_dim(key_mask, part_index * rows, rows).reshape(slots, slot_len)
    places = lax.broadcasted_iota(jnp.int32, (slots, slot_len), 1)
    valid = (places < lengths[:, None]) & ((mask == 1) | (places == 0))
    target = (
        ((places >= splits[:, None]) & (places < lengths[:, None])).astype(F32).reshape(rows, 1)
    )
    gain_mid = norm1_gain.astype(F32)
    shift_mid = norm1_shift.astype(F32)
    gain_out = norm2_gain.astype(F32)
    shift_out = norm2_shift.astype(F32)

    projected = jnp.einsum("rd,cld->crl", hidden_in, w_qkv, preferred_element_type=F32)
    bias_rows = jnp.stack([b_qv[0], jnp.zeros_like(b_qv[0]), b_qv[1]]).astype(F32)
    projected = (projected + bias_rows[:, None, :]).astype(BF16)
    head_shape = (slots, slot_len, heads, HD)
    queries = projected[0].reshape(head_shape)
    key_rows = projected[1].reshape(head_shape)
    value_rows = projected[2].reshape(head_shape)
    scores = jnp.einsum("sqhe,skhe->shqk", queries, key_rows, preferred_element_type=F32) * (
        HD ** (-0.5)
    )
    masked = jnp.where(valid[:, None, None, :], scores, -1e30)
    largest = jnp.max(masked, axis=-1, keepdims=True)
    weights_raw = jnp.exp(masked - largest)
    totals = jnp.sum(weights_raw, axis=-1, keepdims=True)
    probability = weights_raw / totals
    prob_low = probability.astype(BF16)
    context = jnp.einsum("shqk,skhe->sqhe", prob_low, value_rows, preferred_element_type=F32)
    context_rows = context.astype(BF16).reshape(rows, width)
    attn_out = jnp.dot(context_rows, w_out, preferred_element_type=F32)
    first_sum = hidden_in.astype(F32) + attn_out + out_bias.astype(F32)
    mid_rows, mid_normal, mid_inverse = norm_forward(first_sum, gain_mid, shift_mid)
    mid_low = mid_rows.astype(BF16)
    before = jnp.einsum("rd,fd->rf", mid_low, w_up, preferred_element_type=F32) + b_up.astype(F32)
    activated, gelu_slope = gelu_parts(before)
    activated_low = activated.astype(BF16)
    ffn_out = jnp.dot(activated_low, w_down, preferred_element_type=F32)
    second_sum = mid_rows + ffn_out + down_bias.astype(F32)
    out_rows, out_normal, out_inverse = norm_forward(second_sum, gain_out, shift_out)
    layer_out = out_rows.astype(BF16)

    upstream = out_grad.astype(F32) * target
    grad_gain_out = jnp.sum(upstream * out_normal, axis=0)
    grad_shift_out = jnp.sum(upstream, axis=0)
    second_grad = norm_backward(upstream, out_normal, out_inverse, gain_out)
    grad_down_bias = jnp.sum(second_grad, axis=0)
    second_low = second_grad.astype(BF16)
    grad_down = jnp.einsum("rf,rd->fd", activated_low, second_low, preferred_element_type=F32)
    grad_down = lax.psum(lax.psum_scatter(grad_down, "tensor", scatter_dimension=0, tiled=True), "dp")
    activated_grad = jnp.einsum("rd,fd->rf", second_low, w_down, preferred_element_type=F32)
    before_low = (activated_grad * gelu_slope).astype(BF16)
    grad_up = jnp.einsum("rf,rd->fd", before_low, mid_low, preferred_element_type=F32)
    grad_up_bias = jnp.sum(before_low, axis=0, dtype=F32)
    grad_up = lax.psum(lax.psum_scatter(grad_up, "tensor", scatter_dimension=0, tiled=True), "dp")
    grad_up_bias = lax.psum(
        lax.psum_scatter(grad_up_bias, "tensor", scatter_dimension=0, tiled=True), "dp"
    )
    mid_grad = second_grad + jnp.dot(before_low, w_up, preferred_element_type=F32)
    grad_gain_mid = jnp.sum(mid_grad * mid_normal, axis=0)
    grad_shift_mid = jnp.sum(mid_grad, axis=0)
    first_grad = norm_backward(mid_grad, mid_normal, mid_inverse, gain_mid)
    grad_out_bias = jnp.sum(first_grad, axis=0)
    first_low = first_grad.astype(BF16)
    grad_out_weight = jnp.einsum("rl,rd->ld", context_rows, first_low, preferred_element_type=F32)
    grad_out_weight = lax.psum(
        lax.psum_scatter(grad_out_weight, "tensor", scatter_dimension=0, tiled=True), "dp"
    )
    context_grad = (
        jnp.einsum("rd,ld->rl", first_low, w_out, preferred_element_type=F32)
        .astype(BF16)
        .reshape(head_shape)
    )
    prob_grad = jnp.einsum(
        "sqhe,skhe->shqk", context_grad, value_rows, preferred_element_type=F32
    )
    inner_sum = jnp.sum(probability * prob_grad, axis=-1, keepdims=True)
    score_grad = (probability * (prob_grad - inner_sum)).astype(BF16)
    query_grad = jnp.einsum(
        "shqk,skhe->sqhe", score_grad, key_rows, preferred_element_type=F32
    ) * (HD ** (-0.5))
    key_grad = jnp.einsum(
        "shqk,sqhe->skhe", score_grad, queries, preferred_element_type=F32
    ) * (HD ** (-0.5))
    value_grad = jnp.einsum("shqk,sqhe->skhe", prob_low, context_grad, preferred_element_type=F32)
    projected_grad = jnp.stack(
        [
            query_grad.reshape(rows, width),
            key_grad.reshape(rows, width),
            value_grad.reshape(rows, width),
        ]
    ).astype(BF16)
    grad_qkv = jnp.einsum("crl,rd->cld", projected_grad, hidden_in, preferred_element_type=F32)
    bias_sums = jnp.sum(projected_grad, axis=1, dtype=F32)
    grad_qv_bias = jnp.stack([bias_sums[0], bias_sums[2]])
    input_grad = (
        first_grad
        + jnp.einsum("crl,cld->rd", projected_grad, w_qkv, preferred_element_type=F32)
    ).astype(BF16)
    grad_qkv = lax.psum(lax.psum_scatter(grad_qkv, "tensor", scatter_dimension=1, tiled=True), "dp")
    grad_qv_bias = lax.psum(
        lax.psum_scatter(grad_qv_bias, "tensor", scatter_dimension=1, tiled=True), "dp"
    )
    grad_out_bias, grad_gain_mid, grad_shift_mid, grad_down_bias, grad_gain_out, grad_shift_out = (
        lax.psum(
            (
                grad_out_bias,
                grad_gain_mid,
                grad_shift_mid,
                grad_down_bias,
                grad_gain_out,
                grad_shift_out,
            ),
            ("dp", "tensor"),
        )
    )
    return (
        layer_out,
        input_grad,
        grad_qkv,
        grad_qv_bias,
        grad_out_weight,
        grad_out_bias,
        grad_gain_mid,
        grad_shift_mid,
        grad_up,
        grad_up_bias,
        grad_down,
        grad_down_bias,
        grad_gain_out,
        grad_shift_out,
    )


def solution(mesh):
    in_specs = (
        P(("dp", "tensor"), None),
        P(None, "tensor", None),
        P(None, "tensor"),
        P("tensor", None),
        P(),
        P(),
        P(),
        P("tensor", None),
        P("tensor"),
        P("tensor", None),
        P(),
        P(),
        P(),
        P(("dp", "tensor"), None),
        P("dp"),
        P("dp"),
        P("dp"),
    )
    out_specs = (
        P(("dp", "tensor"), None),
        P(("dp", "tensor"), None),
        P(None, "tensor", None),
        P(None, "tensor"),
        P("tensor", None),
        P(),
        P(),
        P(),
        P("tensor", None),
        P("tensor"),
        P("tensor", None),
        P(),
        P(),
        P(),
    )
    return jax.shard_map(body, mesh=mesh, in_specs=in_specs, out_specs=out_specs, check_vma=False)
```

time: 933 us -> 761 us (0.82)
  waiting for transfers between devices: 560 us -> 440 us
  matrix products: 174 us -> 127 us
  blocking collectives: 64.9 us -> 90 us
  local copies, waits for them, and re-layouts: 75.7 us -> 60.4 us
  other arithmetic: 32.5 us -> 18.2 us
    all_gather x4, waiting for transfers between devices: 187 us -> 79.2 us  [the longest x1 34.8 us: body(): w_up = lax.all_gather(up_weight, 'tensor', axis=0, tiled=True)]
    dot_general x68 -> x18, matrix products: 174 us -> 127 us  [the longest x1 12.8 us: body(): jnp.einsum('rd,fd->rf', mid_low, w_up, preferred_element_type=F32)]
    psum x1, waiting for transfers between devices: 196 us -> 161 us  [body(): lax.psum(lax.psum_scatter(grad_qkv, 'tensor', scatter_dimension=1, tiled=...]
    reduce_scatter x4, waiting for transfers between devices: 175 us -> 197 us  [the longest x1 80.6 us: body(): lax.psum_scatter(grad_up, 'tensor', scatter_dimension=0, tiled=True)]
    all_gather x0 -> x2, blocking collectives: none -> 11.5 us  [the longest x1 6 us: body(): b_qv = lax.all_gather(qv_bias, 'tensor', axis=1, tiled=True)]
    reduce_sum x12 -> x2, other arithmetic: 15 us -> 3.55 us  [the longest x1 2.68 us: body(): bias_sums = jnp.sum(projected_grad, axis=1, dtype=F32)]
    unnamed x0 -> x1, blocking collectives: none -> 10.1 us
    another operation x11 -> x7, local copies, waits for them, and re-layouts: 29.1 us -> 19.1 us  [the longest x6 19 us: body(): jnp.stack([query_grad.reshape(rows, width), key_grad.reshape(rows, width)...]
  transfers between devices with their start and end apart: 9 -> 10, of which waited for: 8 -> 8; matrix products, arithmetic and copies ran while one was open for 4% -> 20% of each run, Pallas kernels for 0% -> 0%
where the time goes in v1:
time: 761 us; the launch traced here: 752 us
  waiting for transfers between devices  440 us (58%)
  matrix products  127 us (17%)
  blocking collectives  90 us (12%)
  local copies, waits for them, and re-layouts  60.4 us (8%)
  other arithmetic  18.2 us (2%)
  between operations  15.8 us (2%)
    psum x1, waiting for transfers between devices, body(): lax.psum(lax.psum_scatter(grad_qkv, 'tensor', scatter_dimension=1, tiled=...  161 us
    reduce_scatter x1, waiting for transfers between devices, body(): lax.psum_scatter(grad_up, 'tensor', scatter_dimension=0, tiled=True)  80.6 us
    reduce_scatter x1, waiting for transfers between devices, body(): lax.psum_scatter(grad_down, 'tensor', scatter_dimension=0, tiled=True)  80.5 us
    psum x1, blocking collectives, body(): lax.psum((grad_out_bias, grad_gain_mid, grad_shift_mid, grad_down_bias, g...  45.4 us
    reduce_scatter x1, waiting for transfers between devices, body(): lax.psum_scatter(grad_qkv, 'tensor', scatter_dimension=1, tiled=True)  36 us
    all_gather x1, waiting for transfers between devices, body(): w_up = lax.all_gather(up_weight, 'tensor', axis=0, tiled=True)  34.8 us
    unnamed x83, local copies, waits for them, and re-layouts  28.7 us
    all_gather x1, waiting for transfers between devices, body(): w_down = lax.all_gather(down_weight, 'tensor', axis=0, tiled=True)  26 us
  transfers between devices with their start and end apart: 10, of which 8 were waited for; matrix products, arithmetic and copies ran while one was open for 20% of the time, Pallas kernels for 0%

profile of v1, /device:TPU:0, one launch (start us, length us, event | category | flops | bytes accessed | tf_op | source)
XLA Modules:
  0.0 752.3 jit_solution(9560384906454295733)
XLA Ops:
  10.3 6.0 all-gather
  18.9 5.5 all-gather.1
  26.2 16.9 %all-gather.7.cloned.1.call-done = bf16[3,768,768]{2,1,0:T(8,128)(2,1)} async-done(((bf16[3,192,768]{2,1,0:T(8,128)(2,1)}), bf16[3,768,768]{2,1,0:T(8,128)(2,1)}) %all-gather.7.cloned.1.call-update) | async-done | bytes 3538960 | tf_op jit(solution)/shard_map/all_gather | solution.py:66
  43.2 6.1 fusion.8
  66.4 34.8 %all-gather.11.cloned.1.call-done = bf16[3072,768]{1,0:T(8,128)(2,1)} async-done(((bf16[768,768]{1,0:T(8,128)(2,1)}), bf16[3072,768]{1,0:T(8,128)(2,1)}) %all-gather.11.cloned.1.call-update) | async-done | bytes 4718608 | tf_op jit(solution)/shard_map/all_gather | solution.py:69
  101.2 12.8 %multiply_convert_fusion = (bf16[1024,3072]{1,0:T(8,128)(2,1)}, f32[1024,3072]{1,0:T(8,128)}) fusion(f32[3072]{0:T(1024)S(1)} %bitcast.117, bf16[3072,768]{1,0:T(8,128)(2,1)} %all-gather.11.cloned.1.call-done, f32[1024,768]{0,1:T(8,128)S(1)} %get-tuple-element.92, f32[768]{0:T(1024)S(1)} %convert_element_type.102, f32[768]{0:T(1024)S(1)} %convert_element_type.101, ...), kind=kOutput, calls=%fused_computation.9 | convolution fusion | flops 4854644736 | bytes 26765312 | tf_op jit(solution)/shard_map/rd,fd->rf/dot_general | solution.py:108
  114.1 26.0 %all-gather.13.cloned.1.call-done = bf16[3072,768]{1,0:T(8,128)(2,1)} async-done(((bf16[768,768]{1,0:T(8,128)(2,1)}), bf16[3072,768]{1,0:T(8,128)(2,1)}) %all-gather.13.cloned.1.call-update) | async-done | bytes 4718608 | tf_op jit(solution)/shard_map/all_gather | solution.py:71
  140.1 9.4 %fusion.66 = (f32[1024]{0:T(1024)S(1)}, f32[1024,768]{0,1:T(8,128)S(1)}) fusion(f32[768]{0:T(1024)S(1)} %convert_element_type.106, bf16[1024,3072]{1,0:T(8,128)(2,1)} %get-tuple-element.93, bf16[3072,768]{1,0:T(8,128)(2,1)} %all-gather.13.cloned.1.call-done, f32[768]{0:T(1024)S(1)} %convert_element_type.102, f32[768]{0:T(1024)S(1)} %convert_element_type.101, ...), kind=kOutput, calls=%fused_computation.113 | convolution fusion | flops 4837342208 | bytes 17323008 | tf_op jit(solution)/shard_map/dot_general | solution.py:111
  152.4 12.6 %convert_reduce_fusion = (f32[3072]{0:T(1024)S(1)}, bf16[1024,3072]{1,0:T(8,128)(2,1)}) fusion(f32[1024,3072]{1,0:T(8,128)} %get-tuple-element.94, f32[3072]{0:T(1024)S(1)} %bitcast.118, bf16[3072,768]{1,0:T(8,128)(2,1)S(1)} %copy-done.26, f32[1024]{0:T(1024)S(1)} %get-tuple-element.102, f32[1024,768]{0,1:T(8,128)S(1)} %get-tuple-element.96, ...), kind=kOutput, calls=%fused_computation.8 | convolution fusion | flops 4880593920 | bytes 28359680 | tf_op jit(solution)/shard_map/rd,fd->rf/dot_general | solution.py:124
  165.0 11.2 %multiply_reduce_fusion.2 = (f32[768]{0:T(1024)S(1)}, f32[1024]{0:T(1024)S(1)}, f32[1024]{0:T(1024)S(1)}, f32[768]{0:T(1024)S(1)}, f32[1024,768]{0,1:T(8,128)S(1)}) fusion(f32[1024,768]{0,1:T(8,128)S(1)} %copy-done.6, f32[1024]{0:T(1024)S(1)} %add_rsqrt_fusion.1, f32[1024]{0:T(1024)S(1)} %broadcast_multiply_fusion.5, f32[768]{0:T(1024)S(1)} %convert_element_type.101, ...), kind=kOutput, calls=%fused_computation.23 | convolution fusion | flops 4846776320 | bytes 22069248 | tf_op jit(solution)/shard_map/dot_general | solution.py:132
  191.7 7.5 multiply_reduce_fusion
  199.2 5.0 multiply_convert_fusion.1
  228.1 5.5 fusion.30
  242.3 9.7 %fusion.20 = f32[3,768,768]{2,1,0:T(8,128)} fusion(bf16[1024,768]{1,0:T(8,128)(2,1)} %param.17, bf16[1,1024,768]{2,1,0:T(8,128)(2,1)} %copy.104, bf16[1,1024,768]{2,1,0:T(8,128)(2,1)} %copy.103, bf16[1,1024,768]{2,1,0:T(8,128)(2,1)} %copy.102), kind=kOutput, calls=%fused_computation.58 | convolution fusion | flops 3628597248 | bytes 13369344 | tf_op jit(solution)/shard_map/crl,rd->cld/dot_general | solution.py:166
  252.1 11.7 %fusion.47 = f32[3072,768]{1,0:T(8,128)} fusion(bf16[1024,3072]{1,0:T(8,128)(2,1)} %get-tuple-element.93, bf16[1024,768]{0,1:T(8,128)(2,1)} %copy.88, f32[1024,768]{0,1:T(8,128)S(1)} %get-tuple-element.96, f32[1024]{0:T(1024)S(1)} %get-tuple-element.102, f32[1024]{0:T(1024)S(1)} %get-tuple-element.103, f32[1024]{0:T(1024)S(1)} %get-tuple-element.87, ...), kind=kOutput, calls=%fused_computation.81 | convolution fusion | flops 4839702528 | bytes 20470784 | tf_op jit(solution)/shard_map/rf,rd->fd/dot_general | solution.py:122
  263.9 11.9 %fusion.56 = f32[3072,768]{1,0:T(8,128)} fusion(bf16[1024,3072]{1,0:T(8,128)(2,1)} %get-tuple-element.101, f32[1024,768]{0,1:T(8,128)} %copy-done.5, f32[768]{0:T(1024)S(1)} %convert_element_type.102, f32[768]{0:T(1024)S(1)} %convert_element_type.101, f32[1024]{0:T(1024)S(1)} %add_rsqrt_fusion.1, f32[1024]{0:T(1024)S(1)} %broadcast_multiply_fusion.5), kind=kOutput, calls=%fused_computation.105 | convolution fusion | flops 4835770368 | bytes 18888704 | tf_op jit(solution)/shard_map/rf,rd->fd/dot_general | solution.py:126
  279.6 36.0 %reduce-scatter.8.cloned.1.call-done = f32[3,192,768]{2,1,0:T(8,128)} async-done(((f32[3,768,768]{2,1,0:T(8,128)}), f32[3,192,768]{2,1,0:T(8,128)}) %reduce-scatter.8.cloned.1.call-update) | async-done | bytes 1769488 | tf_op jit(solution)/shard_map/reduce_scatter | solution.py:173
  315.7 80.5 %reduce-scatter.14.cloned.1.call-done = f32[768,768]{1,0:T(8,128)} async-done(((f32[3072,768]{1,0:T(8,128)}), f32[768,768]{1,0:T(8,128)}) %reduce-scatter.14.cloned.1.call-update) | async-done | bytes 2359312 | tf_op jit(solution)/shard_map/reduce_scatter | solution.py:123
  396.2 80.6 %reduce-scatter.12.cloned.1.call-done = f32[768,768]{1,0:T(8,128)} async-done(((f32[3072,768]{1,0:T(8,128)}), f32[768,768]{1,0:T(8,128)}) %reduce-scatter.12.cloned.1.call-update) | async-done | bytes 2359312 | tf_op jit(solution)/shard_map/reduce_scatter | solution.py:128
  478.7 9.3 %fusion.9 = bf16[1024,768]{0,1:T(8,128)(2,1)} fusion(f32[1024,768]{0,1:T(8,128)} %copy-done.8, bf16[3,768,768]{2,1,0:T(8,128)(2,1)} %all-gather.7.cloned.1.call-done, bf16[1,1024,768]{2,1,0:T(8,128)(2,1)} %copy.104, bf16[1,1024,768]{2,1,0:T(8,128)(2,1)} %copy.103, bf16[1,1024,768]{2,1,0:T(8,128)(2,1)} %copy.102), kind=kOutput, calls=%fused_computation.21 | convolution fusion | flops 3630170112 | bytes 12976128 | tf_op jit(solution)/shard_map/crl,cld->rd/dot_general | solution.py:171
  497.5 10.1 %all-reduce = f32[3072]{0:T(1024)S(1)} all-reduce(f32[3072]{0:T(1024)S(1)} %get-tuple-element.100), channel_id=6, replica_groups=mesh['dp'=8,'tensor'=4] {'tensor'}, use_global_device_ids=true, to_apply=%region_27.28.clone | all-reduce | flops 3072 | bytes 24576
  507.6 45.4 %all-reduce.1 = (f32[768]{0:T(1024)}, f32[768]{0:T(1024)}, f32[768]{0:T(1024)}, f32[768]{0:T(1024)}, f32[768]{0:T(1024)}, /*index=5*/f32[768]{0:T(1024)}) all-reduce(f32[768]{0:T(1024)S(1)} %get-tuple-element.77, f32[768]{0:T(1024)S(1)} %get-tuple-element.56, ...), channel_id=1, replica_groups=mesh['dp'=8,'tensor'=4] {'dp','tensor'}, use_global_device_ids=true, to_apply=%region_19.20 | all-reduce | flops 4608 | bytes 36864 | tf_op jit(solution)/shard_map/psum | solution.py:178
  554.0 23.0 %all-reduce.2 = (f32[2,192]{1,0:T(2,128)}, f32[768]{0:T(1024)}) all-reduce(f32[2,192]{1,0:T(2,128)S(1)} %copy.119, f32[768]{0:T(1024)S(1)} %dynamic-slice.1), channel_id=1, replica_groups=mesh['dp'=8,'tensor'=4] {'dp'}, use_global_device_ids=true, to_apply=%region_15.16 | all-reduce | flops 1152 | bytes 9216 | tf_op jit(solution)/shard_map/psum | solution.py:174
  577.0 161.4 %all-reduce.6.cloned.1.call-done = (f32[3,192,768]{2,1,0:T(8,128)}, f32[192,768]{1,0:T(8,128)}, f32[768,768]{1,0:T(8,128)}, f32[768,768]{1,0:T(8,128)}) async-done(((f32[3,192,768]{2,1,0:T(8,128)}, f32[192,768]{1,0:T(8,128)}, f32[768,768]{1,0:T(8,128)}, f32[768,768]{1,0:T(8,128)}), (f32[3,192,768]{2,1,0:T(8,128)}, f32[192,768]{1,0:T(8,128)}, f32[768,768]{1,0:T(8,128)}, ...) | async-done | bytes 7077904 | tf_op jit(solution)/shard_map/psum | solution.py:173
  (156 shorter events, 97.3 us)
Async XLA Ops:
  7.2 10.0 %copy-start.12 = (bf16[1024,768]{1,0:T(8,128)(2,1)S(1)}, bf16[1024,768]{1,0:T(8,128)(2,1)}, u32[]{:S(2)}) copy-start(bf16[1024,768]{1,0:T(8,128)(2,1)} %param.17) | copy-start | bytes 4718596
  7.2 35.9 %all-gather.7.cloned.1.call-start = ((), (), s32[]{:S(2)}) async-start(), calls=%async_computation.5 | async-start | bytes 4423680 | tf_op jit(solution)/shard_map/all_gather | solution.py:66
  8.0 10.9 %copy-start.18 = (bf16[768]{0:T(1024)(128)(2,1)S(1)}, bf16[768]{0:T(1024)(128)(2,1)}, u32[]{:S(2)}) copy-start(bf16[768]{0:T(1024)(128)(2,1)} %param.21) | copy-start | bytes 4612
  8.0 10.9 %copy-start.19 = (bf16[768]{0:T(1024)(128)(2,1)S(1)}, bf16[768]{0:T(1024)(128)(2,1)}, u32[]{:S(2)}) copy-start(bf16[768]{0:T(1024)(128)(2,1)} %param.22) | copy-start | bytes 4612
  8.0 10.9 %copy-start.20 = (bf16[768]{0:T(1024)(128)(2,1)S(1)}, bf16[768]{0:T(1024)(128)(2,1)}, u32[]{:S(2)}) copy-start(bf16[768]{0:T(1024)(128)(2,1)} %param.23) | copy-start | bytes 4612
  8.0 10.9 %copy-start.24 = (bf16[768]{0:T(1024)(128)(2,1)S(1)}, bf16[768]{0:T(1024)(128)(2,1)}, u32[]{:S(2)}) copy-start(bf16[768]{0:T(1024)(128)(2,1)} %param.25) | copy-start | bytes 4612
  8.0 16.4 %copy-start.21 = (bf16[768]{0:T(1024)(128)(2,1)S(1)}, bf16[768]{0:T(1024)(128)(2,1)}, u32[]{:S(2)}) copy-start(bf16[768]{0:T(1024)(128)(2,1)} %param.27) | copy-start | bytes 4612
  8.0 16.4 %copy-start.11 = (bf16[1024,768]{1,0:T(8,128)(2,1)S(1)}, bf16[1024,768]{1,0:T(8,128)(2,1)}, u32[]{:S(2)}) copy-start(bf16[1024,768]{1,0:T(8,128)(2,1)} %param.30) | copy-start | bytes 4718596
  8.0 54.2 %all-gather.9.cloned.1.call-start = ((), (), s32[]{:S(2)}) async-start(), calls=%async_computation.6 | async-start | bytes 1474560 | tf_op jit(solution)/shard_map/all_gather | solution.py:68
  8.8 92.4 %all-gather.11.cloned.1.call-start = ((), (), s32[]{:S(2)}) async-start(), calls=%async_computation.7 | async-start | bytes 5898240 | tf_op jit(solution)/shard_map/all_gather | solution.py:69
  9.5 130.6 %all-gather.13.cloned.1.call-start = ((), (), s32[]{:S(2)}) async-start(), calls=%async_computation.8 | async-start | bytes 5898240 | tf_op jit(solution)/shard_map/all_gather | solution.py:71
  10.1 269.6 %reduce-scatter.10.cloned.1.call-start = ((), (), s32[]{:S(2)}) async-start(), calls=%async_computation.10 | async-start | bytes 2949120 | tf_op jit(solution)/shard_map/reduce_scatter | solution.py:140
  17.2 8.9 %copy-start.22 = (bf16[768]{0:T(1024)(128)(2,1)S(1)}, bf16[768]{0:T(1024)(128)(2,1)}, u32[]{:S(2)}) copy-start(bf16[768]{0:T(1024)(128)(2,1)} %param.28) | copy-start | bytes 4612
  66.0 48.0 %copy-start.5 = (f32[1024,768]{0,1:T(8,128)}, f32[1024,768]{0,1:T(8,128)S(1)}, u32[]{:S(2)}) copy-start(f32[1024,768]{0,1:T(8,128)S(1)} %get-tuple-element.92) | copy-start | bytes 9437188
  152.4 12.6 %copy-start.6 = (f32[1024,768]{0,1:T(8,128)S(1)}, f32[1024,768]{0,1:T(8,128)}, u32[]{:S(2)}) copy-start(f32[1024,768]{0,1:T(8,128)} %copy-done.5) | copy-start | bytes 9437188
  181.9 133.8 %reduce-scatter.8.cloned.1.call-start = ((), (), s32[]{:S(2)}) async-start(), calls=%async_computation.9 | async-start | bytes 8847360 | tf_op jit(solution)/shard_map/reduce_scatter | solution.py:173
  191.6 7.6 %copy-start.16 = (bf16[96,8,8,128]{3,2,1,0:T(8,128)(2,1)}, bf16[96,8,8,128]{3,2,1,0:T(8,128)(2,1)S(1)}, u32[]{:S(2)}) copy-start(bf16[96,8,8,128]{3,2,1,0:T(8,128)(2,1)S(1)} %copy.124) | copy-start | bytes 4718596
  191.7 7.6 %slice-start = ((s8[6291456]{0:T(1024)(128)(4,1)}), s8[4194304]{0:T(1024)(128)(4,1)S(1)}, s32[]{:S(2)}) async-start(s8[6291456]{0:T(1024)(128)(4,1)} %bitcast.106), calls=%async_computation.15 | async-start | bytes 8388608
  191.7 7.5 %slice-start.1 = ((s8[6291456]{0:T(1024)(128)(4,1)}), s8[2097152]{0:T(1024)(128)(4,1)S(1)}, s32[]{:S(2)}) async-start(s8[6291456]{0:T(1024)(128)(4,1)} %bitcast.106), calls=%async_computation.16 | async-start | bytes 4194304
  199.2 5.0 copy-start.3
  252.0 144.2 %reduce-scatter.14.cloned.1.call-start = ((), (), s32[]{:S(2)}) async-start(), calls=%async_computation.12 | async-start | bytes 11796480 | tf_op jit(solution)/shard_map/reduce_scatter | solution.py:123
  263.8 212.9 %reduce-scatter.12.cloned.1.call-start = ((), (), s32[]{:S(2)}) async-start(), calls=%async_computation.11 | async-start | bytes 11796480 | tf_op jit(solution)/shard_map/reduce_scatter | solution.py:128
  275.8 277.2 %reduce-scatter.16.cloned.1.call-start = ((), (), s32[]{:S(2)}) async-start(), calls=%async_computation.13 | async-start | bytes 491520
  279.6 458.8 %all-reduce.6.cloned.1.call-start = ((), (), s32[]{:S(2)}) async-start(), calls=%async_computation.14 | async-start | bytes 14155776 | tf_op jit(solution)/shard_map/psum | solution.py:173
  (18 other events, 41.1 us)
Sparse Core Ops, SparseCore 0:
  9.6 33.5 all-gather.6
  44.7 17.4 all-gather.8
  63.7 37.4 all-gather.10
  102.6 37.4 all-gather.12
  182.0 32.7 reduce-scatter.9
  252.2 63.4 reduce-scatter.7
  318.3 77.8 reduce-scatter.13
  398.8 77.9 reduce-scatter.11
  479.8 20.8 reduce-scatter.15
  505.0 233.3 all-reduce.5
